TPU v7x, 512 devices: a whole 4x4x16 slice. The times are simulated.
512 devices in a mesh: seg: 64 (over y, z_lo, core), blk: 8 (over x, z_hi).
Axes of the slice: x: 4, y: 4, z: 16 (z_hi: 2, z_lo: 8; z = z_hi * 8 + z_lo), core: 2. Of those that a mesh axis runs over, the one named last changes fastest.
Arguments:
- record: float32 [24, 262144], P(None, ('seg', 'blk')), may hold values from -8 to 8, as said below
- templates: bfloat16 [128, 24, 512], P('blk'), may hold values from -6 to 6
Outputs:
- detection: float32 [128, 262144], P(None, ('seg', 'blk'))
Inputs may be any that keep to these rules, and one draw needn't show every extreme that they name: `record`: network samples.
All inputs are finite; a program needn't handle non-finite values.
Results may differ from a plain program's by a relative error of at most 0.0032.
Values may be sent and summed in bfloat16 or wider, within the bound.
No kernel may reach another device: no remote copies, remote signals or barrier semaphores. Data moves between devices by JAX's collectives and lax.ppermute only.
A program may use at most 64 MiB of HBM per device.

v0:
```python
import jax
import jax.numpy as jnp
from jax import lax
from jax.sharding import PartitionSpec as P


def passed_along(block, axis, distance):
    devices = range(lax.axis_size(axis))
    route = [(i - distance, i) for i in devices if i - distance in devices]
    return lax.ppermute(block, axis, route)


def normalize(templates):
    widened = templates.astype(jnp.float32)
    centred = widened - jnp.mean(widened, axis=2, keepdims=True)
    return (centred / jnp.sqrt(jnp.sum(centred * centred, axis=2, keepdims=True) + 1e-06)).astype(
        jnp.bfloat16
    )


def band_matrix(samples, window):
    span = samples + window - 1
    rows = jnp.arange(span, dtype=jnp.int32)[:, None]
    cols = jnp.arange(samples, dtype=jnp.int32)[None, :]
    inside = jnp.logical_and(rows >= cols, rows < cols + window)
    return inside.astype(jnp.float32)


def window_scale(extended, band, window):
    stacked_rows = jnp.concatenate([extended, extended * extended], axis=0)
    sums = jnp.dot(
        stacked_rows, band, precision=lax.Precision.HIGHEST, preferred_element_type=jnp.float32
    )
    channels = extended.shape[0]
    window_sum = sums[:channels]
    window_sq = sums[channels:]
    spread = window_sq - window_sum * window_sum / window
    return 1.0 / jnp.sqrt(jnp.maximum(spread, 1.0))


def correlate(record_bf, kernel_block, scale):
    members = kernel_block.shape[0]
    channels = kernel_block.shape[1]
    window = kernel_block.shape[2]
    samples = scale.shape[1]
    span = record_bf.shape[1]
    kernels = jnp.transpose(kernel_block, (1, 0, 2))

    def one_channel(total, inputs):
        channel_row, kernel_rows, factor = inputs
        repeated = jnp.tile(channel_row, window + 1)[: window * (span + 1)]
        hankel = repeated.reshape(window, span + 1)[:, :samples]
        product = jnp.dot(kernel_rows, hankel, preferred_element_type=jnp.float32)
        return (total + product * factor[None, :], None)

    total, unused = lax.scan(
        one_channel, jnp.zeros((members, samples), jnp.float32), (record_bf, kernels, scale)
    )
    return total / channels


def body(record, templates):
    samples = record.shape[1]
    window = templates.shape[2]
    trailing = passed_along(record, ("seg", "blk"), -1)
    padded_rec = jnp.concatenate([record, trailing], axis=1)
    normalized = normalize(templates)
    band = band_matrix(samples, window)
    extended = padded_rec[:, : samples + window - 1]
    scale = window_scale(extended, band, window)
    record_bf = extended.astype(jnp.bfloat16)
    collected = lax.all_gather(normalized, "blk", axis=0, tiled=True)
    stacked = correlate(record_bf, collected, scale)
    power_sum = lax.psum(jnp.sum(stacked * stacked, axis=1), ("seg", "blk"))
    record_len = samples * lax.axis_size("seg") * lax.axis_size("blk")
    return stacked / jnp.sqrt(power_sum / record_len + 1e-06)[:, None]


def solution(mesh):
    return jax.shard_map(
        body,
        mesh=mesh,
        in_specs=(P(None, ("seg", "blk")), P("blk", None, None)),
        out_specs=P(None, ("seg", "blk")),
        check_vma=False,
    )
```

profile of v0, /device:TPU:1, one launch (start us, length us, event | category | flops | bytes accessed | tf_op | source)
XLA Modules:
  0.0 357.7 jit_solution(17654023932856735463)
XLA Ops:
  9.0 1.9 fusion.12
  11.0 19.0 %collective-permute-start = (f32[24,512]{1,0:T(8,128)}, f32[24,512]{1,0:T(8,128)S(1)}, u32[]{:S(2)}, u32[]{:S(2)}) collective-permute-start(f32[24,512]{1,0:T(8,128)} %param.4), channel_id=1, source_target_pairs={{1,0},{2,1},{3,2},{4,3},{5,4},{6,5},{7,6},{8,7},{9,8},{10,9},{11,1... | collective-permute-start | bytes 147464 | tf_op jit(solution)/shard_map/ppermute | solution.py:10
  32.4 129.1 %all-gather.2.cloned.1.call-done = bf16[128,24,512]{2,0,1:T(8,128)(2,1)} async-done(((bf16[16,24,512]{2,0,1:T(8,128)(2,1)}), bf16[128,24,512]{2,0,1:T(8,128)(2,1)}) %all-gather.2.cloned.1.call-update) | async-done | bytes 3145744 | tf_op jit(solution)/shard_map/all_gather | solution.py:72
  161.6 86.4 %while.11 = (s32[]{:T(128)}, f32[128,512]{1,0:T(8,128)S(1)}, bf16[24,128,512]{2,1,0:T(8,128)(2,1)}, bf16[24,1023]{1,0:T(8,128)(2,1)S(1)}, f32[24,512]{1,0:T(8,128)S(1)}, /*index=5*/s32[]{:T(128)}, s32[]{:T(128)}) while((s32[]{:T(128)}, f32[128,512]{1,0:T(8,128)S(1)}, bf16[24,128,512]{2,1,0:T(8,128)(2,1)}, ...), condition=%wide.region_3.4_spmd.clone, body=%wide.region_2.3_spmd.clone.sunk | while | flops 67305472 | bytes 8535635 | solution.py:56
  161.7 1.6 tile.17
  165.3 1.6 tile.17
  168.9 1.6 tile.17
  172.5 1.6 tile.17
  176.1 1.6 tile.17
  179.7 1.6 tile.17
  183.3 1.6 tile.17
  186.9 1.6 tile.17
  190.5 1.6 tile.17
  194.1 1.6 tile.17
  197.7 1.6 tile.17
  201.3 1.6 tile.17
  204.9 1.6 tile.17
  208.5 1.6 tile.17
  212.1 1.6 tile.17
  219.3 1.6 tile.17
  226.5 1.6 tile.17
  233.7 1.6 tile.17
  240.9 1.6 tile.17
  248.1 102.0 %psum.7 = f32[128]{0:T(128)S(1)} all-reduce(f32[128]{0:T(128)S(1)} %multiply_reduce_fusion), channel_id=1, replica_groups=mesh['seg'=64,'blk'=8] {'seg','blk'}, use_global_device_ids=true, to_apply=%region_5.6 | all-reduce | flops 128 | bytes 1024 | tf_op jit(solution)/shard_map/psum | solution.py:74
  (167 shorter events, 59.5 us)
Async XLA Ops:
  6.5 25.0 %copy-start = (f32[24,512]{1,0:T(8,128)S(1)}, f32[24,512]{1,0:T(8,128)}, u32[]{:S(2)}) copy-start(f32[24,512]{1,0:T(8,128)} %param.4) | copy-start | bytes 147460
  6.5 155.0 %all-gather.2.cloned.1.call-start = ((), (), s32[]{:S(2)}) async-start(), calls=%async_computation | async-start | bytes 3538944 | tf_op jit(solution)/shard_map/all_gather | solution.py:72
  11.0 20.5 %collective-permute-start = (f32[24,512]{1,0:T(8,128)}, f32[24,512]{1,0:T(8,128)S(1)}, u32[]{:S(2)}, u32[]{:S(2)}) collective-permute-start(f32[24,512]{1,0:T(8,128)} %param.4), channel_id=1, source_target_pairs={{1,0},{2,1},{3,2},{4,3},{5,4},{6,5},{7,6},{8,7},{9,8},{10,9},{11,1... | collective-permute-start | bytes 147464 | tf_op jit(solution)/shard_map/ppermute | solution.py:10
Sparse Core Ops, SparseCore 0:
  11.1 150.3 all-gather.1
where the time goes:
time: 358 us
  waiting for transfers between devices  131 us (37%)
  blocking collectives  102 us (28%)
  local copies, waits for them, and re-layouts  56.6 us (16%)
  matrix products  29 us (8%)
  starting transfers between devices  19 us (5%)
  between operations  13.5 us (4%)
  other arithmetic  5.36 us (1%)
    all_gather x1, waiting for transfers between devices, body(): collected = lax.all_gather(normalized, 'blk', axis=0, tiled=True)  129 us
    psum x1, blocking collectives, body(): power_sum = lax.psum(jnp.sum(stacked * stacked, axis=1), ('seg', 'blk'))  102 us
    another operation x48, local copies, waits for them, and re-layouts, one_channel(): repeated = jnp.tile(channel_row, window + 1)[:window * (span + 1)]  42.1 us
    dot_general x24, matrix products, one_channel(): product = jnp.dot(kernel_rows, hankel, preferred_element_type=jnp.float32)  28.2 us
    ppermute x1, starting transfers between devices, passed_along(): return lax.ppermute(block, axis, route)  19 us
    reshape x24, local copies, waits for them, and re-layouts, one_channel(): hankel = repeated.reshape(window, span + 1)[:, :samples]  11.8 us
  transfers between devices with their start and end apart: 2, of which 2 were waited for; matrix products, arithmetic and copies ran while one was open for 0% of the time, Pallas kernels for 0%

commit v1 on v0

--- a/solution.py
+++ b/solution.py
@@ -71,7 +71,7 @@
     record_bf = extended.astype(jnp.bfloat16)
     collected = lax.all_gather(normalized, "blk", axis=0, tiled=True)
     stacked = correlate(record_bf, collected, scale)
-    power_sum = lax.psum(jnp.sum(stacked * stacked, axis=1), ("seg", "blk"))
+    power_sum = lax.psum(lax.psum(jnp.sum(stacked * stacked, axis=1), "seg"), "blk")
     record_len = samples * lax.axis_size("seg") * lax.axis_size("blk")
     return stacked / jnp.sqrt(power_sum / record_len + 1e-06)[:, None]
 

time: 358 us -> 507 us (1.42); the launches traced: 358 us -> 498 us
  blocking collectives: 102 us -> 242 us
    psum x1 -> x2, blocking collectives: 102 us -> 242 us  [the longest x1 212 us: body(): lax.psum(jnp.sum(stacked * stacked, axis=1), 'seg')]
where the time goes in v1:
time: 507 us; the launch traced here: 498 us
  blocking collectives  242 us (48%)
  waiting for transfers between devices  131 us (26%)
  local copies, waits for them, and re-layouts  56.6 us (11%)
  matrix products  29 us (6%)
  starting transfers between devices  19 us (4%)
  between operations  13.5 us (3%)
  other arithmetic  5.36 us (1%)
    psum x1, blocking collectives, body(): lax.psum(jnp.sum(stacked * stacked, axis=1), 'seg')  212 us
    all_gather x1, waiting for transfers between devices, body(): collected = lax.all_gather(normalized, 'blk', axis=0, tiled=True)  129 us
    another operation x48, local copies, waits for them, and re-layouts, one_channel(): repeated = jnp.tile(channel_row, window + 1)[:window * (span + 1)]  42.1 us
    psum x1, blocking collectives, body(): lax.psum(lax.psum(jnp.sum(stacked * stacked, axis=1), 'seg'), 'blk')  30.1 us
    dot_general x24, matrix products, one_channel(): product = jnp.dot(kernel_rows, hankel, preferred_element_type=jnp.float32)  28.2 us
    ppermute x1, starting transfers between devices, passed_along(): return lax.ppermute(block, axis, route)  19 us
    reshape x24, local copies, waits for them, and re-layouts, one_channel(): hankel = repeated.reshape(window, span + 1)[:, :samples]  11.8 us
  transfers between devices with their start and end apart: 2, of which 2 were waited for; matrix products, arithmetic and copies ran while one was open for 0% of the time, Pallas kernels for 0%

profile of v1, /device:TPU:1, one launch (start us, length us, event | category | flops | bytes accessed | tf_op | source)
XLA Modules:
  0.0 498.2 jit_solution(573375563152777427)
XLA Ops:
  9.0 1.9 fusion.12
  11.0 19.0 %collective-permute-start = (f32[24,512]{1,0:T(8,128)}, f32[24,512]{1,0:T(8,128)S(1)}, u32[]{:S(2)}, u32[]{:S(2)}) collective-permute-start(f32[24,512]{1,0:T(8,128)} %param.4), channel_id=1, source_target_pairs={{1,0},{2,1},{3,2},{4,3},{5,4},{6,5},{7,6},{8,7},{9,8},{10,9},{11,1... | collective-permute-start | bytes 147464 | tf_op jit(solution)/shard_map/ppermute | solution.py:10
  32.4 129.1 %all-gather.2.cloned.1.call-done = bf16[128,24,512]{2,0,1:T(8,128)(2,1)} async-done(((bf16[16,24,512]{2,0,1:T(8,128)(2,1)}), bf16[128,24,512]{2,0,1:T(8,128)(2,1)}) %all-gather.2.cloned.1.call-update) | async-done | bytes 3145744 | tf_op jit(solution)/shard_map/all_gather | solution.py:72
  161.6 86.4 %while.11 = (s32[]{:T(128)}, f32[128,512]{1,0:T(8,128)S(1)}, bf16[24,128,512]{2,1,0:T(8,128)(2,1)}, bf16[24,1023]{1,0:T(8,128)(2,1)S(1)}, f32[24,512]{1,0:T(8,128)S(1)}, /*index=5*/s32[]{:T(128)}, s32[]{:T(128)}) while((s32[]{:T(128)}, f32[128,512]{1,0:T(8,128)S(1)}, bf16[24,128,512]{2,1,0:T(8,128)(2,1)}, ...), condition=%wide.region_3.4_spmd.clone, body=%wide.region_2.3_spmd.clone.sunk | while | flops 67305472 | bytes 8535635 | solution.py:56
  161.7 1.6 tile.17
  165.3 1.6 tile.17
  168.9 1.6 tile.17
  172.5 1.6 tile.17
  176.1 1.6 tile.17
  179.7 1.6 tile.17
  183.3 1.6 tile.17
  186.9 1.6 tile.17
  190.5 1.6 tile.17
  194.1 1.6 tile.17
  197.7 1.6 tile.17
  201.3 1.6 tile.17
  204.9 1.6 tile.17
  212.1 1.6 tile.17
  219.3 1.6 tile.17
  226.5 1.6 tile.17
  233.7 1.6 tile.17
  240.9 1.6 tile.17
  248.1 212.4 %psum.14 = f32[128]{0:T(128)S(1)} all-reduce(f32[128]{0:T(128)S(1)} %multiply_reduce_fusion), channel_id=1, replica_groups=mesh['seg'=64,'blk'=8] {'seg'}, use_global_device_ids=true, to_apply=%region_5.6 | all-reduce | flops 128 | bytes 1024 | tf_op jit(solution)/shard_map/psum | solution.py:74
  460.5 30.1 %psum.15 = f32[128]{0:T(128)S(1)} all-reduce(f32[128]{0:T(128)S(1)} %psum.14), channel_id=1, replica_groups=mesh['seg'=64,'blk'=8] {'blk'}, use_global_device_ids=true, to_apply=%region_6.7 | all-reduce | flops 128 | bytes 1024 | tf_op jit(solution)/shard_map/psum | solution.py:74
  (168 shorter events, 61.1 us)
Async XLA Ops:
  6.5 25.0 %copy-start = (f32[24,512]{1,0:T(8,128)S(1)}, f32[24,512]{1,0:T(8,128)}, u32[]{:S(2)}) copy-start(f32[24,512]{1,0:T(8,128)} %param.4) | copy-start | bytes 147460
  6.5 155.0 %all-gather.2.cloned.1.call-start = ((), (), s32[]{:S(2)}) async-start(), calls=%async_computation | async-start | bytes 3538944 | tf_op jit(solution)/shard_map/all_gather | solution.py:72
  11.0 20.5 %collective-permute-start = (f32[24,512]{1,0:T(8,128)}, f32[24,512]{1,0:T(8,128)S(1)}, u32[]{:S(2)}, u32[]{:S(2)}) collective-permute-start(f32[24,512]{1,0:T(8,128)} %param.4), channel_id=1, source_target_pairs={{1,0},{2,1},{3,2},{4,3},{5,4},{6,5},{7,6},{8,7},{9,8},{10,9},{11,1... | collective-permute-start | bytes 147464 | tf_op jit(solution)/shard_map/ppermute | solution.py:10
Sparse Core Ops, SparseCore 0:
  11.1 150.3 all-gather.1
